TPU v7x, 512 devices: a whole 4x8x8 slice. The times are simulated.
512 devices in a mesh: row: 32 (over z, y_lo), col: 16 (over y_hi, x, core).
Axes of the slice: x: 4, y: 8 (y_hi: 2, y_lo: 4; y = y_hi * 4 + y_lo), z: 8, core: 2. Of those that a mesh axis runs over, the one named last changes fastest.
Arguments:
- group_store: bfloat16 [512, 32, 1600], P('row'), may hold values from -6 to 6
- positions: bfloat16 [320, 1600], replicated, may hold values from -6 to 6
- ln_gain: bfloat16 [1600], replicated, may hold values from 0.099609375 to 1.8984375
- w_query: bfloat16 [1600, 1600], P('row', 'col'), may hold values from -6 to 6
- w_keyval: bfloat16 [1600, 2, 1600], P('row', None, 'col'), may hold values from -6 to 6
- w_out: bfloat16 [1600, 1600], P('col', 'row'), may hold values from -0.3125 to 0.3125
- group_src: int32 [128, 10], replicated, may hold values from 0 to 511, as said below
- lengths: int32 [32, 4], replicated, may hold values from 1 to 10, as said below
- selected: int32 [128, 32], replicated, may hold values from 0 to 319, as said below
Outputs:
- joined_cache: bfloat16 [128, 320, 2, 1600], P('row', None, None, 'col')
- hidden_out: bfloat16 [128, 32, 1600], P('row', None, 'col')
Inputs may be any that keep to these rules, and one draw needn't show every extreme that they name: `group_src`: exactly 32 of the 40 entries of the requests of one row device name a group held by another device, and at most 2 of them name any one other device; some device reaches 2 in every draw. `lengths`: every row device has a request with all 10 groups live. `selected`: each row holds 32 distinct places in increasing order, all below 32 times the request's live groups.
All inputs are finite; a program needn't handle non-finite values.
Results may differ from a plain program's by a relative error of at most 0.015.
Values may be sent and summed in bfloat16 or wider, within the bound.
No kernel may reach another device: no remote copies, remote signals or barrier semaphores. Data moves between devices by JAX's collectives and lax.ppermute only.
A program may use at most 64 MiB of HBM per device.

v0:
```python
import jax
import jax.numpy as jnp
from jax import lax
from jax.sharding import PartitionSpec as P

HEADS = 25
HEAD_DIM = 64
REM_DEV = 32


def joined(part, axis, combine):
    gathered = jax.tree.map(lambda a: lax.all_gather(a, axis), part)

    def take(source):
        return jax.tree.map(lambda a: lax.dynamic_index_in_dim(a, source, 0, False), gathered)

    return lax.fori_loop(
        1, lax.axis_size(axis), lambda source, state: combine(state, take(source)), take(0)
    )


def layer_norm(shifted, ln_gain):
    center = shifted - jnp.mean(shifted, axis=-1, keepdims=True)
    spread = jnp.mean(center * center, axis=-1, keepdims=True)
    return center * lax.rsqrt(spread + 1e-05) * ln_gain.astype(jnp.float32)


def blend(earlier, later):
    top_one, total_one, summed_one = earlier
    top_two, total_two, summed_two = later
    joint = jnp.maximum(top_one, top_two)
    scale_one = jnp.exp(top_one - joint)
    scale_two = jnp.exp(top_two - joint)
    totals = total_one * scale_one + total_two * scale_two
    summed = summed_one * scale_one[:, :, None] + summed_two * scale_two[:, :, None]
    return (joint, totals, summed)


def per_device(
    group_store, positions, ln_gain, w_query, w_keyval, w_out, group_src, lengths, selected
):
    row_count = lax.axis_size("row")
    col_count = lax.axis_size("col")
    row_index = lax.axis_index("row")
    col_index = lax.axis_index("col")
    slot_count, group_len, full_width = group_store.shape
    narrow = full_width // col_count
    req_here = lengths.shape[1]
    group_count = group_src.shape[1]
    ref_count = req_here * group_count
    token_span = group_count * group_len
    sel_count = selected.shape[1]
    query_count = req_here * sel_count
    remote_most = REM_DEV
    capacity = max(2, (remote_most + row_count - 2) // (row_count - 1))
    owner_src = group_src.reshape(row_count, ref_count)
    holder_all = owner_src // slot_count
    slot_all = owner_src % slot_count
    owner_ids = jnp.arange(row_count, dtype=jnp.int32)
    wanted = jnp.ones((row_count, ref_count), dtype=jnp.bool_)
    remote_all = (holder_all != owner_ids[:, None]) & wanted
    outgoing = remote_all & (holder_all == row_index)
    out_rank = jnp.cumsum(outgoing.astype(jnp.int32), axis=1) - 1
    slot_ids = jnp.arange(capacity, dtype=jnp.int32)
    chosen = outgoing[:, None, :] & (out_rank[:, None, :] == slot_ids[None, :, None])
    send_slot = jnp.sum(jnp.where(chosen, slot_all[:, None, :], 0), axis=2)
    send_live = jnp.any(chosen, axis=2)
    my_holder = lax.dynamic_index_in_dim(holder_all, row_index, 0, keepdims=False)
    my_slot = lax.dynamic_index_in_dim(slot_all, row_index, 0, keepdims=False)
    my_remote = lax.dynamic_index_in_dim(remote_all, row_index, 0, keepdims=False)
    incoming = (my_holder[None, :] == owner_ids[:, None]) & my_remote[None, :]
    in_rank = jnp.cumsum(incoming.astype(jnp.int32), axis=1) - 1
    my_rank = jnp.sum(jnp.where(incoming, in_rank, 0), axis=0)
    flat_index = my_holder * capacity + my_rank
    ordinal = jnp.cumsum(my_remote.astype(jnp.int32)) - 1
    compact_ids = jnp.arange(remote_most, dtype=jnp.int32)
    compact_pick = my_remote[None, :] & (ordinal[None, :] == compact_ids[:, None])
    compact_index = jnp.sum(jnp.where(compact_pick, flat_index[None, :], 0), axis=1)
    compact_live = jnp.any(compact_pick, axis=1)
    payload = group_store[send_slot]
    received = lax.all_to_all(
        jnp.where(send_live[:, :, None, None], payload, jnp.zeros_like(payload)),
        "row",
        split_axis=0,
        concat_axis=0,
        tiled=True,
    )
    flat = received.reshape(row_count * capacity, group_len, received.shape[-1])
    gathered_rows = flat[compact_index]
    fetched = jnp.where(compact_live[:, None, None], gathered_rows, jnp.zeros_like(gathered_rows))
    query_rows, keyval_rows, out_cols = (
        lax.all_gather(w_query, "row", axis=0, tiled=True),
        lax.all_gather(w_keyval, "row", axis=0, tiled=True),
        lax.all_gather(w_out, "row", axis=1, tiled=True),
    )
    pos_global = positions.astype(jnp.float32)
    pos_local = jnp.tile(pos_global[:group_len], (group_count, 1))
    my_lengths = lax.dynamic_index_in_dim(lengths, row_index, 0, keepdims=False)
    my_picked = lax.dynamic_slice_in_dim(selected, row_index * req_here, req_here, 0)
    ordinal_req = jnp.clip(ordinal, 0, remote_most - 1).reshape(req_here, group_count)
    remote_req = my_remote.reshape(req_here, group_count)
    slot_req = my_slot.reshape(req_here, group_count)
    token_place = jnp.arange(token_span, dtype=jnp.int32)

    def one_request(inputs):
        live_count, picked, remote_row, ordinal_row, slot_row = inputs
        groups = jnp.where(remote_row[:, None, None], fetched[ordinal_row], group_store[slot_row])
        cached = groups.reshape(token_span, full_width)
        shifted = cached.astype(jnp.float32) + pos_global - pos_local
        normed = layer_norm(shifted, ln_gain).astype(jnp.bfloat16)
        keyval = jnp.einsum(
            "td,dsc->tsc", normed, keyval_rows, preferred_element_type=jnp.float32
        ).astype(jnp.bfloat16)
        alive = token_place < live_count * group_len
        keyval = jnp.where(alive[:, None, None], keyval, jnp.zeros_like(keyval))
        return (keyval, shifted[picked], normed[picked])

    joined_cache, picked_shift, picked_norm = lax.map(
        one_request, (my_lengths, my_picked, remote_req, ordinal_req, slot_req)
    )
    queries = jnp.dot(
        picked_norm.reshape(query_count, full_width), query_rows, preferred_element_type=jnp.float32
    ).astype(jnp.bfloat16)
    query_full = lax.all_gather(queries, "col", axis=1, tiled=True)
    block_len = req_here * token_span // col_count
    key_block = lax.all_to_all(
        joined_cache.reshape(req_here * token_span, 2, narrow),
        "col",
        split_axis=0,
        concat_axis=2,
        tiled=True,
    )
    key_place = col_index * block_len + jnp.arange(block_len, dtype=jnp.int32)
    key_req = key_place // token_span
    key_pos = key_place % token_span
    query_req = jnp.arange(query_count, dtype=jnp.int32) // sel_count
    query_pos = my_picked.reshape(query_count)
    allowed = (query_req[:, None] == key_req[None, :]) & (key_pos[None, :] <= query_pos[:, None])
    query_heads = query_full.astype(jnp.float32).reshape(query_count, HEADS, HEAD_DIM)
    key_heads = key_block[:, 0].astype(jnp.float32).reshape(block_len, HEADS, HEAD_DIM)
    value_heads = key_block[:, 1].astype(jnp.float32).reshape(block_len, HEADS, HEAD_DIM)
    scores = jnp.einsum("qhe,khe->hqk", query_heads, key_heads) * 0.125
    scores = jnp.where(allowed[None], scores, -1e30)
    local_top = jnp.max(scores, axis=-1)
    weights = jnp.where(allowed[None], jnp.exp(scores - local_top[:, :, None]), 0.0)
    summed = jnp.einsum("hqk,khe->hqe", weights, value_heads)
    joint_top, totals, summed = joined((local_top, jnp.sum(weights, axis=-1), summed), "col", blend)
    whole = (summed / totals[:, :, None]).transpose(1, 0, 2).reshape(query_count, full_width)
    attended = lax.dynamic_slice_in_dim(whole, col_index * narrow, narrow, 1).astype(jnp.bfloat16)
    projected = jnp.dot(attended, out_cols, preferred_element_type=jnp.float32)
    own_out = lax.psum_scatter(
        projected.astype(jnp.bfloat16), "col", scatter_dimension=1, tiled=True
    ).astype(jnp.float32)
    own_shift = lax.dynamic_slice_in_dim(
        picked_shift.reshape(query_count, full_width), col_index * narrow, narrow, 1
    )
    hidden_out = (own_shift + own_out).astype(jnp.bfloat16).reshape(req_here, sel_count, narrow)
    return (joined_cache, hidden_out)


def solution(mesh):
    return jax.shard_map(
        per_device,
        mesh=mesh,
        in_specs=(
            P("row", None, None),
            P(),
            P(),
            P("row", "col"),
            P("row", None, "col"),
            P("col", "row"),
            P(),
            P(),
            P(),
        ),
        out_specs=(P("row", None, None, "col"), P("row", None, "col")),
        check_vma=False,
    )
```

profile of v0, /device:TPU:240, one launch (start us, length us, event | category | flops | bytes accessed | tf_op | source)
XLA Modules:
  0.0 885.9 jit_solution(15602323697913155838)
XLA Ops:
  8.9 5.6 gather_fusion.4
  14.4 6.4 broadcast_select_fusion
  20.8 10.4 %all-to-all-start = ((bf16[32,2,32,1600]{3,2,1,0:T(8,128)(2,1)}), bf16[32,2,32,1600]{3,2,1,0:T(8,128)(2,1)}, u32[]{:S(2)}, u32[]{:S(2)}) async-start(bf16[32,2,32,1600]{3,2,1,0:T(8,128)(2,1)} %broadcast_select_fusion), calls=%async_computation | async-start | bytes 13631488 | tf_op jit(solution)/shard_map/all_to_all | solution.py:81
  34.7 298.4 %all_gather.30 = bf16[1600,2,100]{2,1,0:T(2,128)(2,1)S(1)} all-gather(bf16[50,2,100]{2,1,0:T(2,128)(2,1)S(1)} %copy-done.10), channel_id=1, replica_groups=mesh['row'=32,'col'=16] {'row'}, dimensions={0}, use_global_device_ids=true | all-gather | bytes 660000 | tf_op jit(solution)/shard_map/all_gather | solution.py:93
  335.3 4.0 gather_fusion.5
  341.4 52.0 %while.35 = (s32[]{:T(128)}, bf16[4,320,2,100]{1,3,2,0:T(8,128)(2,1)}, f32[4,32,1600]{2,1,0:T(8,128)}, bf16[4,32,1600]{2,1,0:T(8,128)(2,1)}, s32[4]{0:T(128)S(1)...) while((s32[]{:T(128)}, ...), condition=%wide.region_11.12_spmd.clone, body=%wide.region_8.11_spmd.clone.sunk | while | flops 211077472 | bytes 36389364 | solution.py:118
  396.4 9.7 %all-to-all-start.1 = ((bf16[1280,2,100]{2,1,0:T(2,128)(2,1)}), bf16[1280,2,100]{2,1,0:T(2,128)(2,1)S(1)}, u32[]{:S(2)}, u32[]{:S(2)}) async-start(bf16[1280,2,100]{2,1,0:T(2,128)(2,1)} %bitcast.20), calls=%async_computation.1 | async-start | bytes 1310720 | tf_op jit(solution)/shard_map/all_to_all | solution.py:126
  406.2 84.7 %all-gather.3 = bf16[32,50,100]{2,1,0:T(8,128)(2,1)S(1)} all-gather(bf16[1,50,100]{2,1,0:T(8,128)(2,1)S(1)} %bitcast.168), channel_id=1, replica_groups=mesh['row'=32,'col'=16] {'row'}, dimensions={0}, use_global_device_ids=true | all-gather | bytes 330000 | tf_op jit(solution)/shard_map/all_gather | solution.py:92
  491.5 33.3 %all-gather.4 = bf16[16,100,128]{2,1,0:T(8,128)(2,1)S(1)} all-gather(bf16[1,100,128]{2,1,0:T(8,128)(2,1)S(1)} %fusion.19), channel_id=1, replica_groups=mesh['row'=32,'col'=16] {'col'}, dimensions={0}, use_global_device_ids=true | all-gather | bytes 435200 | tf_op jit(solution)/shard_map/all_gather | solution.py:124
  528.1 137.6 %all-gather.7 = bf16[32,50,100]{2,1,0:T(8,128)(2,1)S(1)} all-gather(bf16[1,50,100]{2,1,0:T(8,128)(2,1)S(1)} %bitcast.169), channel_id=1, replica_groups=mesh['row'=32,'col'=16] {'row'}, dimensions={0}, use_global_device_ids=true | all-gather | bytes 330000 | tf_op jit(solution)/shard_map/all_gather | solution.py:94
  666.9 32.6 %all-gather.6 = f32[16,25,128]{2,1,0:T(8,128)} all-gather(f32[1,25,128]{2,1,0:T(8,128)S(1)} %bitcast.166), channel_id=3, replica_groups=mesh['row'=32,'col'=16] {'col'}, dimensions={0}, use_global_device_ids=true | all-gather | bytes 217600 | tf_op jit(solution)/shard_map/all_gather | solution.py:12
  699.4 26.3 %all-gather.5 = f32[16,25,128]{2,1,0:T(8,128)} all-gather(f32[1,25,128]{2,1,0:T(8,128)S(1)} %bitcast.165), channel_id=2, replica_groups=mesh['row'=32,'col'=16] {'col'}, dimensions={0}, use_global_device_ids=true | all-gather | bytes 217600 | tf_op jit(solution)/shard_map/all_gather | solution.py:12
  730.0 83.4 %while.34 = (s32[]{:T(128)}, f32[25,128]{1,0:T(8,128)S(1)}, f32[25,128]{1,0:T(8,128)S(1)}, f32[25,128,64]{2,1,0:T(8,128)}, f32[16,25,128]{2,1,0:T(8,128)}, /*ind...) while((s32[]{:T(128)}, f32[25,128]{1,0:T(8,128)S(1)}, ...), condition=%wide.region_15.16_spmd, body=%wide.region_14.15_spmd.sunk | while | flops 633605 | bytes 5862551 | solution.py:17
  732.5 3.1 fusion.63
  738.1 3.1 fusion.63
  743.6 3.1 fusion.63
  749.2 3.1 fusion.63
  754.7 3.1 fusion.63
  760.3 3.1 fusion.63
  765.9 3.1 fusion.63
  771.4 3.1 fusion.63
  777.0 3.1 fusion.63
  815.8 47.4 %fusion.4 = bf16[128,112]{0,1:T(8,128)(2,1)S(1)} fusion(bf16[128,1600]{0,1:T(8,128)(2,1)S(1)} %convolution_convert_fusion.1), kind=kCustom, calls=%all-reduce-scatter | all-reduce-scatter fusion | flops 229377 | bytes 440320
  870.3 6.5 collective-permute-done.1
  (277 shorter events, 137.5 us)
Async XLA Ops:
  7.2 27.2 %copy-start = (s32[128,32]{0,1:T(8,128)S(1)}, s32[128,32]{0,1:T(8,128)}, u32[]{:S(2)}) copy-start(s32[128,32]{0,1:T(8,128)} %param.21) | copy-start | bytes 49156
  20.8 10.5 %copy-start.6 = (bf16[320,1600]{1,0:T(8,128)(2,1)S(1)}, bf16[320,1600]{1,0:T(8,128)(2,1)}, u32[]{:S(2)}) copy-start(bf16[320,1600]{1,0:T(8,128)(2,1)} %param.14) | copy-start | bytes 3072004
  20.8 314.5 %all-to-all-start = ((bf16[32,2,32,1600]{3,2,1,0:T(8,128)(2,1)}), bf16[32,2,32,1600]{3,2,1,0:T(8,128)(2,1)}, u32[]{:S(2)}, u32[]{:S(2)}) async-start(bf16[32,2,32,1600]{3,2,1,0:T(8,128)(2,1)} %broadcast_select_fusion), calls=%async_computation | async-start | bytes 13631488 | tf_op jit(solution)/shard_map/all_to_all | solution.py:81
  31.2 3.3 copy-start.13
  31.2 3.5 copy-start.10
  339.3 2.1 copy-start.9
  346.4 1.6 copy-start.2
  348.8 1.6 copy-start.7
  359.4 1.6 copy-start.2
  361.8 1.6 copy-start.7
  372.5 1.6 copy-start.2
  374.8 1.6 copy-start.7
  385.5 1.6 copy-start.2
  387.9 1.6 copy-start.7
  393.4 12.8 %copy-start.11 = (bf16[50,100]{1,0:T(8,128)(2,1)S(1)}, bf16[50,100]{1,0:T(8,128)(2,1)}, u32[]{:S(2)}) copy-start(bf16[50,100]{1,0:T(8,128)(2,1)} %param.16) | copy-start | bytes 30004
  393.4 97.8 %copy-start.8 = (bf16[4,32,1600]{2,1,0:T(8,128)(2,1)S(1)}, bf16[4,32,1600]{2,1,0:T(8,128)(2,1)}, u32[]{:S(2)}) copy-start(bf16[4,32,1600]{2,1,0:T(8,128)(2,1)} %get-tuple-element.265) | copy-start | bytes 1228804
  396.4 128.5 %all-to-all-start.1 = ((bf16[1280,2,100]{2,1,0:T(2,128)(2,1)}), bf16[1280,2,100]{2,1,0:T(2,128)(2,1)S(1)}, u32[]{:S(2)}, u32[]{:S(2)}) async-start(bf16[1280,2,100]{2,1,0:T(2,128)(2,1)} %bitcast.20), calls=%async_computation.1 | async-start | bytes 1310720 | tf_op jit(solution)/shard_map/all_to_all | solution.py:126
  406.1 321.1 %all-gather.10.cloned.1.call-start = ((), (), s32[]{:S(2)}) async-start(), calls=%async_computation.2 | async-start | bytes 13926400 | tf_op jit(solution)/shard_map/all_gather | solution.py:12
  526.5 1.6 copy-start.12
  813.4 2.1 copy-start.5
  813.4 55.6 %copy-start.4 = (bf16[4,320,2,100]{1,3,2,0:T(8,128)(2,1)S(1)}, bf16[4,320,2,100]{1,3,2,0:T(8,128)(2,1)}, u32[]{:S(2)}) copy-start(bf16[4,320,2,100]{1,3,2,0:T(8,128)(2,1)} %get-tuple-element.366) | copy-start | bytes 1536004
  815.4 63.7 %copy-start.1 = (s32[128,32]{0,1:T(8,128)S(1)}, s32[128,32]{0,1:T(8,128)}, u32[]{:S(2)}) copy-start(s32[128,32]{0,1:T(8,128)} %param.21) | copy-start | bytes 49156
  863.2 13.6 %collective-permute-start = (bf16[128,112]{0,1:T(8,128)(2,1)S(1)}, bf16[128,112]{0,1:T(8,128)(2,1)S(1)}, u32[]{:S(2)}, u32[]{:S(2)}) collective-permute-start(bf16[128,112]{0,1:T(8,128)(2,1)S(1)} %fusion.4), channel_id=1, source_target_pairs={{0,1},{1,2},{2,3},{3,4},{4,5},{5,6},{6,7},{7,8},{8,9},{9,10},{10,1... | collective-permute-start | bytes 86024
  865.2 11.7 %collective-permute-start.1 = (bf16[128,68]{0,1:T(8,128)(2,1)S(1)}, bf16[128,68]{0,1:T(8,128)(2,1)S(1)}, u32[]{:S(2)}, u32[]{:S(2)}) collective-permute-start(bf16[128,68]{0,1:T(8,128)(2,1)S(1)} %slice.38), channel_id=1, source_target_pairs={{0,2},{1,3},{2,4},{3,5},{4,6},{5,7},{6,8},{7,9},{8,10},{9,11},{10,... | collective-permute-start | bytes 52232
  (5 other events, 4.9 us)
Sparse Core Ops, SparseCore 0:
  528.2 154.1 all-gather.9
where the time goes:
time: 889 us; the launch traced here: 886 us
  blocking collectives  660 us (74%)
  local copies, waits for them, and re-layouts  93.1 us (10%)
  other arithmetic  76.9 us (9%)
  starting transfers between devices  24 us (3%)
  between operations  15.1 us (2%)
    all_gather x1, blocking collectives, per_device(): lax.all_gather(w_keyval, 'row', axis=0, tiled=True)  298 us
    all_gather x1, blocking collectives, per_device(): lax.all_gather(w_out, 'row', axis=1, tiled=True)  138 us
    all_gather x1, blocking collectives, per_device(): lax.all_gather(w_query, 'row', axis=0, tiled=True)  84.7 us
    all_gather x2, blocking collectives, joined(): gathered = jax.tree.map(lambda a: lax.all_gather(a, axis), part)  58.9 us
    unnamed x1, blocking collectives  47.4 us
    add x15, other arithmetic, blend(): summed_one * scale_one[:, :, None] + summed_two * scale_two[:, :, None]  46.4 us
    all_gather x1, blocking collectives, per_device(): query_full = lax.all_gather(queries, 'col', axis=1, tiled=True)  33.3 us
    dynamic_slice x34, local copies, waits for them, and re-layouts, take(): lax.dynamic_index_in_dim(a, source, 0, False)  28.2 us
  transfers between devices with their start and end apart: 5, of which 1 were waited for; matrix products, arithmetic and copies ran while one was open for 1% of the time, Pallas kernels for 0%

commit v1 on v0

v1 whole, which is shorter than its diff:
```python
import jax
import jax.numpy as jnp
from jax import lax
from jax.sharding import PartitionSpec as P

HEADS = 25
HEAD_DIM = 64
REM_DEV = 32
ROW_RUN = 4
HIGH = lax.Precision.HIGHEST


def layer_norm(shifted, ln_gain):
    center = shifted - jnp.mean(shifted, axis=-1, keepdims=True)
    spread = jnp.mean(center * center, axis=-1, keepdims=True)
    return center * lax.rsqrt(spread + 1e-05) * ln_gain.astype(jnp.float32)


def row_gather(block, row_count):
    run = ROW_RUN if row_count % ROW_RUN == 0 else 1
    runs = row_count // run
    inner = [block] + [
        lax.ppermute(block, "row", [(z * run + a, z * run + (a + s) % run) for z in range(runs) for a in range(run)])
        for s in range(1, run)
    ]
    stage = jnp.stack(inner)
    outer = [stage] + [
        lax.ppermute(stage, "row", [(z * run + a, ((z + s) % runs) * run + a) for z in range(runs) for a in range(run)])
        for s in range(1, runs)
    ]
    stacked = jnp.stack(outer)
    me = lax.axis_index("row")
    z, a = me // run, me % run
    src_z = (z - jnp.arange(runs)) % runs
    src_a = (a - jnp.arange(run)) % run
    order_z = jnp.argsort(src_z)
    order_a = jnp.argsort(src_a)
    ordered = stacked[order_z][:, order_a]
    return ordered.reshape((row_count,) + block.shape)


def gather_weights(w_query, w_keyval, w_out, row_count):
    q_rows, q_cols = w_query.shape
    o_rows, o_cols = w_out.shape
    pack = jnp.concatenate([w_query.reshape(-1), w_keyval.reshape(-1), w_out.reshape(-1)])
    allw = row_gather(pack, row_count)
    q_size = w_query.size
    kv_size = w_keyval.size
    query_rows = allw[:, :q_size].reshape(row_count * q_rows, q_cols)
    keyval_rows = allw[:, q_size:q_size + kv_size].reshape(row_count * q_rows, 2, q_cols)
    out_cols = (
        allw[:, q_size + kv_size:]
        .reshape(row_count, o_rows, o_cols)
        .transpose(1, 0, 2)
        .reshape(o_rows, row_count * o_cols)
    )
    return query_rows, keyval_rows, out_cols


def fetch_groups(group_store, group_src, row_count, row_index, req_here):
    slot_count = group_store.shape[0]
    group_count = group_src.shape[1]
    ref_count = req_here * group_count
    capacity = max(2, (REM_DEV + row_count - 2) // (row_count - 1))
    owner_src = group_src.reshape(row_count, ref_count)
    holder_all = owner_src // slot_count
    slot_all = owner_src % slot_count
    owner_ids = jnp.arange(row_count, dtype=jnp.int32)
    remote_all = holder_all != owner_ids[:, None]
    outgoing = remote_all & (holder_all == row_index)
    out_rank = jnp.cumsum(outgoing.astype(jnp.int32), axis=1) - 1
    slot_ids = jnp.arange(capacity, dtype=jnp.int32)
    chosen = outgoing[:, None, :] & (out_rank[:, None, :] == slot_ids[None, :, None])
    send_slot = jnp.sum(jnp.where(chosen, slot_all[:, None, :], 0), axis=2)
    send_live = jnp.any(chosen, axis=2)
    my_holder = lax.dynamic_index_in_dim(holder_all, row_index, 0, keepdims=False)
    my_slot = lax.dynamic_index_in_dim(slot_all, row_index, 0, keepdims=False)
    my_remote = lax.dynamic_index_in_dim(remote_all, row_index, 0, keepdims=False)
    incoming = (my_holder[None, :] == owner_ids[:, None]) & my_remote[None, :]
    in_rank = jnp.cumsum(incoming.astype(jnp.int32), axis=1) - 1
    my_rank = jnp.sum(jnp.where(incoming, in_rank, 0), axis=0)
    flat_index = my_holder * capacity + my_rank
    payload = group_store[send_slot]
    received = lax.all_to_all(
        jnp.where(send_live[:, :, None, None], payload, jnp.zeros_like(payload)),
        "row",
        split_axis=0,
        concat_axis=0,
        tiled=True,
    )
    flat = received.reshape((row_count * capacity,) + group_store.shape[1:])
    far = flat[jnp.where(my_remote, flat_index, 0)]
    near = group_store[my_slot]
    return jnp.where(my_remote[:, None, None], far, near)


def per_device(
    group_store, positions, ln_gain, w_query, w_keyval, w_out, group_src, lengths, selected
):
    row_count = lax.axis_size("row")
    col_count = lax.axis_size("col")
    row_index = lax.axis_index("row")
    col_index = lax.axis_index("col")
    slot_count, group_len, full_width = group_store.shape
    narrow = full_width // col_count
    req_here = lengths.shape[1]
    group_count = group_src.shape[1]
    token_span = group_count * group_len
    sel_count = selected.shape[1]
    query_count = req_here * sel_count

    query_rows, keyval_rows, out_cols = gather_weights(w_query, w_keyval, w_out, row_count)
    groups = fetch_groups(group_store, group_src, row_count, row_index, req_here)

    pos_global = positions.astype(jnp.float32)
    pos_local = jnp.tile(pos_global[:group_len], (group_count, 1))
    cached = groups.reshape(req_here, token_span, full_width)
    shifted = cached.astype(jnp.float32) + pos_global - pos_local
    normed = layer_norm(shifted, ln_gain).astype(jnp.bfloat16)

    my_lengths = lax.dynamic_index_in_dim(lengths, row_index, 0, keepdims=False)
    my_picked = lax.dynamic_slice_in_dim(selected, row_index * req_here, req_here, 0)
    token_place = jnp.arange(token_span, dtype=jnp.int32)

    keyval = jnp.einsum(
        "btd,dsc->btsc", normed, keyval_rows, preferred_element_type=jnp.float32
    ).astype(jnp.bfloat16)
    alive = token_place[None, :] < (my_lengths * group_len)[:, None]
    joined_cache = jnp.where(alive[:, :, None, None], keyval, jnp.zeros_like(keyval))

    req_ids = jnp.arange(req_here, dtype=jnp.int32)[:, None]
    picked_norm = normed[req_ids, my_picked]
    queries = jnp.einsum(
        "bid,dc->bic", picked_norm, query_rows, preferred_element_type=jnp.float32
    ).astype(jnp.bfloat16)

    first_feature = col_index * narrow
    feature_head = (first_feature + jnp.arange(narrow, dtype=jnp.int32)) // HEAD_DIM
    first_head = first_feature // HEAD_DIM
    last_piece = (first_feature + narrow - 1) // HEAD_DIM - first_head
    piece_count = (narrow + 2 * HEAD_DIM - 2) // HEAD_DIM
    query_f = queries.astype(jnp.float32)
    key_f = joined_cache[:, :, 0].astype(jnp.float32)
    value_f = joined_cache[:, :, 1].astype(jnp.float32)
    masks = [feature_head == first_head + p for p in range(piece_count)]
    partial = [
        jnp.einsum(
            "bie,bte->bit", jnp.where(m[None, None, :], query_f, 0.0), key_f, precision=HIGH
        )
        for m in masks
    ]
    right_piece = partial[0]
    for p in range(1, piece_count):
        right_piece = jnp.where(last_piece == p, partial[p], right_piece)
    from_left = lax.ppermute(right_piece, "col", [(i, i + 1) for i in range(col_count - 1)])
    from_right = lax.ppermute(partial[0], "col", [(i + 1, i) for i in range(col_count - 1)])
    allowed = token_place[None, None, :] <= my_picked[:, :, None]
    attended = jnp.zeros((req_here, sel_count, narrow), jnp.float32)
    for p in range(piece_count):
        full = partial[p]
        if p == 0:
            full = full + from_left
        full = full + jnp.where(last_piece == p, from_right, 0.0)
        scores = jnp.where(allowed, full * 0.125, -1e30)
        highest = jnp.max(scores, axis=-1, keepdims=True)
        weights = jnp.where(allowed, jnp.exp(scores - highest), 0.0)
        totals = jnp.sum(weights, axis=-1)
        summed = jnp.einsum("bit,bte->bie", weights, value_f, precision=HIGH)
        attended = jnp.where(masks[p][None, None, :], summed / totals[:, :, None], attended)
    attended = attended.astype(jnp.bfloat16).reshape(query_count, narrow)

    projected = jnp.dot(attended, out_cols, preferred_element_type=jnp.float32)
    projected = projected.reshape(query_count, col_count, narrow).transpose(1, 0, 2)
    own_out = jnp.sum(lax.all_to_all(projected, "col", 0, 0, tiled=True), axis=0)
    picked_shift = shifted[req_ids, my_picked]
    own_shift = lax.dynamic_slice_in_dim(
        picked_shift.reshape(query_count, full_width), first_feature, narrow, 1
    )
    hidden_out = (own_shift + own_out).astype(jnp.bfloat16).reshape(req_here, sel_count, narrow)
    return (joined_cache, hidden_out)


def solution(mesh):
    return jax.shard_map(
        per_device,
        mesh=mesh,
        in_specs=(
            P("row", None, None),
            P(),
            P(),
            P("row", "col"),
            P("row", None, "col"),
            P("col", "row"),
            P(),
            P(),
            P(),
        ),
        out_specs=(P("row", None, None, "col"), P("row", None, "col")),
        check_vma=False,
    )
```

time: 889 us -> 367 us (0.41)
  the two profiles are of different devices: /device:TPU:240 before, /device:TPU:1 now
where the time goes in v1:
time: 367 us; the launch traced here: 366 us
  waiting for transfers between devices  179 us (49%)
  starting transfers between devices  80.4 us (22%)
  local copies, waits for them, and re-layouts  57.8 us (16%)
  other arithmetic  38.8 us (11%)
  matrix products  8.53 us (2%)
    ppermute x7, waiting for transfers between devices, row_gather(): lax.ppermute(stage, 'row', [(z * run + a, (z + s) % runs * run + a) for z...  165 us
    all_to_all x1, starting transfers between devices, per_device(): lax.all_to_all(projected, 'col', 0, 0, tiled=True)  27.6 us
    ppermute x7, starting transfers between devices, row_gather(): lax.ppermute(stage, 'row', [(z * run + a, (z + s) % runs * run + a) for z...  23.1 us
    all_to_all x1, starting transfers between devices, fetch_groups(): lax.all_to_all(jnp.where(send_live[:, :, None, None], payload, jnp.zeros_...  13.2 us
    all_to_all x1, waiting for transfers between devices, per_device(): lax.all_to_all(projected, 'col', 0, 0, tiled=True)  12.8 us
    convert_element_type x2, other arithmetic, per_device(): normed = layer_norm(shifted, ln_gain).astype(jnp.bfloat16)  12.5 us
    ppermute x3, starting transfers between devices, row_gather(): lax.ppermute(block, 'row', [(z * run + a, z * run + (a + s) % run) for z...  10.3 us
    gather x4, local copies, waits for them, and re-layouts, row_gather(): ordered = stacked[order_z][:, order_a]  10 us
  transfers between devices with their start and end apart: 14, of which 5 were waited for; matrix products, arithmetic and copies ran while one was open for 14% of the time, Pallas kernels for 0%

profile of v1, /device:TPU:1, one launch (start us, length us, event | category | flops | bytes accessed | tf_op | source)
XLA Modules:
  0.0 365.9 jit_solution(2274013253062462525)
XLA Ops:
  3.6 6.1 %collective-permute-start.2 = (bf16[20000]{0:T(1024)(128)(2,1)S(1)}, bf16[20000]{0:T(1024)(128)(2,1)S(1)}, u32[]{:S(2)}, u32[]{:S(2)}) collective-permute-start(bf16[20000]{0:T(1024)(128)(2,1)S(1)} %concatenate.7), channel_id=1, source_target_pairs={{0,48},{16,0},{32,16},{48,32},{64,112},{80,64},{96,80},{112,96},{1... | collective-permute-start | bytes 120008 | tf_op jit(solution)/shard_map/ppermute | solution.py:23
  16.5 4.0 %gather_fusion = bf16[64,32,1600]{2,1,0:T(8,128)(2,1)} fusion(bf16[16,32,1600]{2,1,0:T(8,128)(2,1)S(1)} %copy-done, s32[1024]{0:T(1024)S(1)} %get-tuple-element.48), kind=kCustom, calls=%fused_computation | custom fusion | bytes 13107456 | tf_op jit(solution)/shard_map/gather | solution.py:83
  20.5 6.4 %broadcast_select_fusion = bf16[32,2,32,1600]{3,2,1,0:T(8,128)(2,1)} fusion(bf16[32,2,32,1600]{3,2,1,0:T(8,128)(2,1)} %bitcast.114, pred[32,2]{1,0:T(8,128)(4,1)S(1)} %copy.59), kind=kLoop, calls=%fused_computation.11 | loop fusion | flops 3276800 | bytes 13107264 | tf_op jit(solution)/shard_map/jit(_where)/select_n | solution.py:85
  27.0 13.2 %all-to-all-start = ((bf16[32,2,32,1600]{3,2,1,0:T(8,128)(2,1)}), bf16[32,2,32,1600]{3,2,1,0:T(8,128)(2,1)}, u32[]{:S(2)}, u32[]{:S(2)}) async-start(bf16[32,2,32,1600]{3,2,1,0:T(8,128)(2,1)} %broadcast_select_fusion), calls=%async_computation | async-start | bytes 13631488 | tf_op jit(solution)/shard_map/all_to_all | solution.py:84
  43.3 3.1 collective-permute-start.3
  48.9 3.3 gather_fusion.2
  52.3 4.4 %collective-permute-start.8 = (bf16[4,20000]{1,0:T(4,128)(2,1)S(1)}, bf16[4,20000]{1,0:T(4,128)(2,1)S(1)}, u32[]{:S(2)}, u32[]{:S(2)}) collective-permute-start(bf16[4,20000]{1,0:T(4,128)(2,1)S(1)} %get-tuple-element.28), channel_id=1, source_target_pairs={{0,384},{16,400},{32,416},{48,432},{64,448},{80,464},{96,480},{112... | collective-permute-start | bytes 480008 | tf_op jit(solution)/shard_map/ppermute | solution.py:28
  56.7 6.0 %collective-permute-start.7 = (bf16[4,20000]{1,0:T(4,128)(2,1)S(1)}, bf16[4,20000]{1,0:T(4,128)(2,1)S(1)}, u32[]{:S(2)}, u32[]{:S(2)}) collective-permute-start(bf16[4,20000]{1,0:T(4,128)(2,1)S(1)} %get-tuple-element.28), channel_id=1, source_target_pairs={{0,320},{16,336},{32,352},{48,368},{64,384},{80,400},{96,416},{112... | collective-permute-start | bytes 480008 | tf_op jit(solution)/shard_map/ppermute | solution.py:28
  64.9 3.7 %collective-permute-start.5 = (bf16[4,20000]{1,0:T(4,128)(2,1)S(1)}, bf16[4,20000]{1,0:T(4,128)(2,1)S(1)}, u32[]{:S(2)}, u32[]{:S(2)}) collective-permute-start(bf16[4,20000]{1,0:T(4,128)(2,1)S(1)} %get-tuple-element.28), channel_id=1, source_target_pairs={{0,192},{16,208},{32,224},{48,240},{64,256},{80,272},{96,288},{112... | collective-permute-start | bytes 480008 | tf_op jit(solution)/shard_map/ppermute | solution.py:28
  68.6 121.1 %collective-permute-done.3 = bf16[4,20000]{1,0:T(4,128)(2,1)S(1)} collective-permute-done((bf16[4,20000]{1,0:T(4,128)(2,1)S(1)}, bf16[4,20000]{1,0:T(4,128)(2,1)S(1)}, u32[]{:S(2)}, u32[]{:S(2)}) %collective-permute-start.3) | collective-permute-done | bytes 160032 | tf_op jit(solution)/shard_map/ppermute | solution.py:28
  192.3 40.5 %collective-permute-done.4 = bf16[4,20000]{1,0:T(4,128)(2,1)S(1)} collective-permute-done((bf16[4,20000]{1,0:T(4,128)(2,1)S(1)}, bf16[4,20000]{1,0:T(4,128)(2,1)S(1)}, u32[]{:S(2)}, u32[]{:S(2)}) %collective-permute-start.4) | collective-permute-done | bytes 160032 | tf_op jit(solution)/shard_map/ppermute | solution.py:28
  238.4 3.3 collective-permute-done.9
  242.5 3.9 %gather_fusion.3 = bf16[8,4,20000]{2,1,0:T(4,128)(2,1)} fusion(bf16[8,4,20000]{2,1,0:T(4,128)(2,1)} %bitcast_dynamic-update-slice_fusion, s32[1024]{0:T(1024)S(1)} %pad_clamp_fusion.1), kind=kCustom, calls=%fused_computation.3 | custom fusion | bytes 2560032 | tf_op jit(solution)/shard_map/gather | solution.py:38
  256.0 3.6 copy.64
  260.6 6.4 %gather_fusion.1 = bf16[40,32,1600]{2,1,0:T(8,128)(2,1)} fusion(bf16[64,32,1600]{2,1,0:T(8,128)(2,1)} %bitcast.2, s32[1024]{0:T(1024)S(1)} %get-tuple-element.50), kind=kCustom, calls=%fused_computation.1 | custom fusion | bytes 8192160 | tf_op jit(solution)/shard_map/gather | solution.py:92
  267.1 7.9 %fusion.58 = (f32[4,320]{1,0:T(4,128)S(1)}, f32[4,320,1600]{2,1,0:T(8,128)}) fusion(f32[320,1600]{1,0:T(8,128)S(1)} %bitcast.115, f32[320,1600]{1,0:T(8,128)} %convert_element_type.70, pred[4,320]{1,0:T(4,128)(4,1)S(1)} %broadcast_in_dim.173, bf16[4,320,1600]{2,1,0:T(8,128)(2,1)} %bitcast.106, bf16[4,320,1600]{2,1,0:T(8,128)(2,1)} %bitcast.109), kind=kLoop, calls=%fused_computation.145 | loop fusion | flops 10238720 | bytes 20486400 | tf_op jit(solution)/shard_map/reduce_sum | solution.py:14
  275.1 4.4 %multiply_reduce_fusion = f32[4,320]{1,0:T(4,128)S(1)} fusion(f32[4,320,1600]{2,1,0:T(8,128)} %get-tuple-element.30, f32[4,320]{1,0:T(4,128)S(1)} %broadcast_multiply_fusion), kind=kLoop, calls=%fused_computation.9 | loop fusion | flops 6142720 | bytes 8202240 | tf_op jit(solution)/shard_map/reduce_sum | solution.py:15
  279.6 5.5 %multiply_convert_fusion = bf16[4,320,1600]{2,1,0:T(8,128)(2,1)} fusion(f32[4,320,1600]{2,1,0:T(8,128)} %get-tuple-element.30, f32[1600]{0:T(1024)S(1)} %convert_element_type.72, f32[4,320]{1,0:T(4,128)S(1)} %add_rsqrt_fusion, f32[4,320]{1,0:T(4,128)S(1)} %broadcast_multiply_fusion), kind=kLoop, calls=%fused_computation.7 | loop fusion | flops 8192000 | bytes 12304640 | tf_op jit(solution)/shard_map/convert_element_type | solution.py:119
  290.3 3.8 %add.221 = f32[4,320,1600]{2,1,0:T(8,128)} broadcast(bf16[320,1600]{1,0:T(8,128)(2,1)S(1)} %copy-done.3), dimensions={1,2} | broadcast | bytes 9216000 | tf_op jit(solution)/shard_map/add | solution.py:118
  294.1 7.0 %multiply_convert_fusion.1 = bf16[40,32,1600]{2,1,0:T(8,128)(2,1)} fusion(f32[40,32,1600]{2,1,0:T(8,128)S(1)} %bitcast.112, f32[40,32,1600]{2,1,0:T(8,128)} %bitcast.113, f32[1600]{0:T(1024)S(1)} %convert_element_type.72, f32[40,32]{1,0:T(8,128)S(1)} %rsqrt.13, f32[40,32]{1,0:T(8,128)S(1)} %div.83, bf16[40,32,1600]{2,1,0:T(8,128)(2,1)S(1)} %bitcast.111, ...), kind=kLoop, calls=%fused_computation.8 | loop fusion | flops 16384000 | bytes 28689920 | tf_op jit(solution)/shard_map/convert_element_type | solution.py:119
  301.2 3.8 %fusion = bf16[4,320,2,100]{1,3,2,0:T(8,128)(2,1)S(1)} fusion(bf16[4,320,1600,1]{2,1,3,0:T(8,128)(2,1)} %bitcast.118, bf16[1600,2,100]{0,2,1:T(8,128)(2,1)S(1)} %copy-done.5, pred[4,320]{1,0:T(4,128)(4,1)S(1)} %iota_compare_fusion.4), kind=kOutput, calls=%fused_computation.15 | convolution fusion | flops 819712000 | bytes 5249280 | tf_op jit(solution)/shard_map/btd,dsc->btsc/dot_general | solution.py:125
  319.0 27.6 %all-to-all-start.1 = ((f32[16,128,100]{1,2,0:T(8,128)}), f32[16,128,100]{1,2,0:T(8,128)S(1)}, u32[]{:S(2)}, u32[]{:S(2)}) async-start(f32[16,128,100]{1,2,0:T(8,128)} %convolution_bitcast_fusion), calls=%async_computation.1 | async-start | bytes 1703936 | tf_op jit(solution)/shard_map/all_to_all | solution.py:174
  346.7 3.4 gather_fusion.5
  351.4 12.8 %all-to-all-done.1 = f32[16,128,100]{1,2,0:T(8,128)S(1)} async-done(((f32[16,128,100]{1,2,0:T(8,128)}), f32[16,128,100]{1,2,0:T(8,128)S(1)}, u32[]{:S(2)}, u32[]{:S(2)}) %all-to-all-start.1) | async-done | bytes 819232 | tf_op jit(solution)/shard_map/all_to_all | solution.py:174
  (142 shorter events, 59.4 us)
Async XLA Ops:
  0.6 15.8 %copy-start = (bf16[16,32,1600]{2,1,0:T(8,128)(2,1)S(1)}, bf16[16,32,1600]{2,1,0:T(8,128)(2,1)}, u32[]{:S(2)}) copy-start(bf16[16,32,1600]{2,1,0:T(8,128)(2,1)} %param.9) | copy-start | bytes 4915204
  3.6 38.5 %collective-permute-start.2 = (bf16[20000]{0:T(1024)(128)(2,1)S(1)}, bf16[20000]{0:T(1024)(128)(2,1)S(1)}, u32[]{:S(2)}, u32[]{:S(2)}) collective-permute-start(bf16[20000]{0:T(1024)(128)(2,1)S(1)} %concatenate.7), channel_id=1, source_target_pairs={{0,48},{16,0},{32,16},{48,32},{64,112},{80,64},{96,80},{112,96},{1... | collective-permute-start | bytes 120008 | tf_op jit(solution)/shard_map/ppermute | solution.py:23
  9.7 32.5 %collective-permute-start.1 = (bf16[20000]{0:T(1024)(128)(2,1)S(1)}, bf16[20000]{0:T(1024)(128)(2,1)S(1)}, u32[]{:S(2)}, u32[]{:S(2)}) collective-permute-start(bf16[20000]{0:T(1024)(128)(2,1)S(1)} %concatenate.7), channel_id=1, source_target_pairs={{0,32},{16,48},{32,0},{48,16},{64,96},{80,112},{96,64},{112,80},{1... | collective-permute-start | bytes 120008 | tf_op jit(solution)/shard_map/ppermute | solution.py:23
  11.6 30.6 %collective-permute-start = (bf16[20000]{0:T(1024)(128)(2,1)S(1)}, bf16[20000]{0:T(1024)(128)(2,1)S(1)}, u32[]{:S(2)}, u32[]{:S(2)}) collective-permute-start(bf16[20000]{0:T(1024)(128)(2,1)S(1)} %concatenate.7), channel_id=1, source_target_pairs={{0,16},{16,32},{32,48},{48,0},{64,80},{80,96},{96,112},{112,64},{1... | collective-permute-start | bytes 120008 | tf_op jit(solution)/shard_map/ppermute | solution.py:23
  26.9 13.3 %copy-start.8 = (s32[32,4]{0,1:T(4,128)S(1)}, s32[32,4]{0,1:T(4,128)}, u32[]{:S(2)}) copy-start(s32[32,4]{0,1:T(4,128)} %param.16) | copy-start | bytes 1540
  26.9 14.6 %copy-start.6 = (s32[128,32]{0,1:T(8,128)S(1)}, s32[128,32]{0,1:T(8,128)}, u32[]{:S(2)}) copy-start(s32[128,32]{0,1:T(8,128)} %param.17) | copy-start | bytes 49156
  27.0 19.7 %copy-start.3 = (bf16[320,1600]{1,0:T(8,128)(2,1)S(1)}, bf16[320,1600]{1,0:T(8,128)(2,1)}, u32[]{:S(2)}) copy-start(bf16[320,1600]{1,0:T(8,128)(2,1)} %param.10) | copy-start | bytes 3072004
  27.0 233.6 %all-to-all-start = ((bf16[32,2,32,1600]{3,2,1,0:T(8,128)(2,1)}), bf16[32,2,32,1600]{3,2,1,0:T(8,128)(2,1)}, u32[]{:S(2)}, u32[]{:S(2)}) async-start(bf16[32,2,32,1600]{3,2,1,0:T(8,128)(2,1)} %broadcast_select_fusion), calls=%async_computation | async-start | bytes 13631488 | tf_op jit(solution)/shard_map/all_to_all | solution.py:84
  40.2 8.7 %copy-start.7 = (bf16[1600]{0:T(1024)(128)(2,1)S(1)}, bf16[1600]{0:T(1024)(128)(2,1)}, u32[]{:S(2)}) copy-start(bf16[1600]{0:T(1024)(128)(2,1)} %param.11) | copy-start | bytes 9604
  43.3 146.4 %collective-permute-start.3 = (bf16[4,20000]{1,0:T(4,128)(2,1)S(1)}, bf16[4,20000]{1,0:T(4,128)(2,1)S(1)}, u32[]{:S(2)}, u32[]{:S(2)}) collective-permute-start(bf16[4,20000]{1,0:T(4,128)(2,1)S(1)} %get-tuple-element.28), channel_id=1, source_target_pairs={{0,64},{16,80},{32,96},{48,112},{64,128},{80,144},{96,160},{112,17... | collective-permute-start | bytes 480008 | tf_op jit(solution)/shard_map/ppermute | solution.py:28
  52.3 185.4 %collective-permute-start.8 = (bf16[4,20000]{1,0:T(4,128)(2,1)S(1)}, bf16[4,20000]{1,0:T(4,128)(2,1)S(1)}, u32[]{:S(2)}, u32[]{:S(2)}) collective-permute-start(bf16[4,20000]{1,0:T(4,128)(2,1)S(1)} %get-tuple-element.28), channel_id=1, source_target_pairs={{0,384},{16,400},{32,416},{48,432},{64,448},{80,464},{96,480},{112... | collective-permute-start | bytes 480008 | tf_op jit(solution)/shard_map/ppermute | solution.py:28
  56.7 180.3 %collective-permute-start.7 = (bf16[4,20000]{1,0:T(4,128)(2,1)S(1)}, bf16[4,20000]{1,0:T(4,128)(2,1)S(1)}, u32[]{:S(2)}, u32[]{:S(2)}) collective-permute-start(bf16[4,20000]{1,0:T(4,128)(2,1)S(1)} %get-tuple-element.28), channel_id=1, source_target_pairs={{0,320},{16,336},{32,352},{48,368},{64,384},{80,400},{96,416},{112... | collective-permute-start | bytes 480008 | tf_op jit(solution)/shard_map/ppermute | solution.py:28
  62.7 173.5 %collective-permute-start.6 = (bf16[4,20000]{1,0:T(4,128)(2,1)S(1)}, bf16[4,20000]{1,0:T(4,128)(2,1)S(1)}, u32[]{:S(2)}, u32[]{:S(2)}) collective-permute-start(bf16[4,20000]{1,0:T(4,128)(2,1)S(1)} %get-tuple-element.28), channel_id=1, source_target_pairs={{0,256},{16,272},{32,288},{48,304},{64,320},{80,336},{96,352},{112... | collective-permute-start | bytes 480008 | tf_op jit(solution)/shard_map/ppermute | solution.py:28
  64.9 170.5 %collective-permute-start.5 = (bf16[4,20000]{1,0:T(4,128)(2,1)S(1)}, bf16[4,20000]{1,0:T(4,128)(2,1)S(1)}, u32[]{:S(2)}, u32[]{:S(2)}) collective-permute-start(bf16[4,20000]{1,0:T(4,128)(2,1)S(1)} %get-tuple-element.28), channel_id=1, source_target_pairs={{0,192},{16,208},{32,224},{48,240},{64,256},{80,272},{96,288},{112... | collective-permute-start | bytes 480008 | tf_op jit(solution)/shard_map/ppermute | solution.py:28
  189.7 43.1 %collective-permute-start.4 = (bf16[4,20000]{1,0:T(4,128)(2,1)S(1)}, bf16[4,20000]{1,0:T(4,128)(2,1)S(1)}, u32[]{:S(2)}, u32[]{:S(2)}) collective-permute-start(bf16[4,20000]{1,0:T(4,128)(2,1)S(1)} %get-tuple-element.28), channel_id=1, source_target_pairs={{0,128},{16,144},{32,160},{48,176},{64,192},{80,208},{96,224},{112... | collective-permute-start | bytes 480008 | tf_op jit(solution)/shard_map/ppermute | solution.py:28
  232.8 8.9 %collective-permute-start.9 = (bf16[4,20000]{1,0:T(4,128)(2,1)S(1)}, bf16[4,20000]{1,0:T(4,128)(2,1)S(1)}, u32[]{:S(2)}, u32[]{:S(2)}) collective-permute-start(bf16[4,20000]{1,0:T(4,128)(2,1)S(1)} %get-tuple-element.28), channel_id=1, source_target_pairs={{0,448},{16,464},{32,480},{48,496},{64,0},{80,16},{96,32},{112,48}... | collective-permute-start | bytes 480008 | tf_op jit(solution)/shard_map/ppermute | solution.py:28
  267.1 7.9 %copy-start.2 = (f32[10,32,1600]{2,1,0:T(8,128)}, f32[10,32,1600]{2,1,0:T(8,128)S(1)}, u32[]{:S(2)}) copy-start(f32[10,32,1600]{2,1,0:T(8,128)S(1)} %tile.8) | copy-start | bytes 6144004
  285.0 9.0 %slice-start = ((s8[4259840]{0:T(1024)(128)(4,1)}), s8[65536]{0:T(1024)(128)(4,1)S(1)}, s32[]{:S(2)}) async-start(s8[4259840]{0:T(1024)(128)(4,1)} %bitcast.107), calls=%async_computation.2 | async-start | bytes 131072
  287.7 6.4 %slice-start.2 = ((s8[4259840]{0:T(1024)(128)(4,1)}), s8[4194304]{0:T(1024)(128)(4,1)S(1)}, s32[]{:S(2)}) async-start(s8[4259840]{0:T(1024)(128)(4,1)} %bitcast.110), calls=%async_computation.4 | async-start | bytes 8388608
  294.1 7.1 %copy-start.5 = (bf16[1600,2,100]{0,2,1:T(8,128)(2,1)S(1)}, bf16[1600,2,100]{0,2,1:T(8,128)(2,1)}, u32[]{:S(2)}) copy-start(bf16[1600,2,100]{0,2,1:T(8,128)(2,1)} %copy.64) | copy-start | bytes 1920004
  305.6 8.7 %collective-permute-start.10 = (f32[4,32,320]{2,1,0:T(8,128)S(1)}, f32[4,32,320]{2,1,0:T(8,128)S(1)}, u32[]{:S(2)}, u32[]{:S(2)}) collective-permute-start(f32[4,32,320]{2,1,0:T(8,128)S(1)} %fusion.9), channel_id=1, source_target_pairs={{1,0},{2,1},{3,2},{4,3},{5,4},{6,5},{7,6},{8,7},{9,8},{10,9},{11,1... | collective-permute-start | bytes 491528 | tf_op jit(solution)/shard_map/ppermute | solution.py:156
  309.6 5.9 %collective-permute-start.11 = (f32[4,32,320]{2,1,0:T(8,128)}, f32[4,32,320]{2,1,0:T(8,128)S(1)}, u32[]{:S(2)}, u32[]{:S(2)}) collective-permute-start(f32[4,32,320]{2,1,0:T(8,128)} %get-tuple-element.43), channel_id=1, source_target_pairs={{0,1},{1,2},{2,3},{3,4},{4,5},{5,6},{6,7},{7,8},{8,9},{9,10},{10,1... | collective-permute-start | bytes 491528 | tf_op jit(solution)/shard_map/ppermute | solution.py:155
  319.0 45.1 %all-to-all-start.1 = ((f32[16,128,100]{1,2,0:T(8,128)}), f32[16,128,100]{1,2,0:T(8,128)S(1)}, u32[]{:S(2)}, u32[]{:S(2)}) async-start(f32[16,128,100]{1,2,0:T(8,128)} %convolution_bitcast_fusion), calls=%async_computation.1 | async-start | bytes 1703936 | tf_op jit(solution)/shard_map/all_to_all | solution.py:174
  346.7 19.3 %copy-start.1 = (bf16[16,32,1600]{2,1,0:T(8,128)(2,1)S(1)}, bf16[16,32,1600]{2,1,0:T(8,128)(2,1)}, u32[]{:S(2)}) copy-start(bf16[16,32,1600]{2,1,0:T(8,128)(2,1)} %param.9) | copy-start | bytes 4915204
  (3 other events, 18.7 us)

commit v2 on v1

--- a/solution.py
+++ b/solution.py
@@ -7,6 +7,7 @@
 HEAD_DIM = 64
 REM_DEV = 32
 ROW_RUN = 4
+FEATURE_SPLIT = 4
 HIGH = lax.Precision.HIGHEST
 
 
@@ -57,8 +58,8 @@
     return query_rows, keyval_rows, out_cols
 
 
-def fetch_groups(group_store, group_src, row_count, row_index, req_here):
-    slot_count = group_store.shape[0]
+def fetch_groups(group_store, group_src, row_count, row_index, col_count, col_index, req_here):
+    slot_count, group_len, full_width = group_store.shape
     group_count = group_src.shape[1]
     ref_count = req_here * group_count
     capacity = max(2, (REM_DEV + row_count - 2) // (row_count - 1))
@@ -80,7 +81,19 @@
     in_rank = jnp.cumsum(incoming.astype(jnp.int32), axis=1) - 1
     my_rank = jnp.sum(jnp.where(incoming, in_rank, 0), axis=0)
     flat_index = my_holder * capacity + my_rank
-    payload = group_store[send_slot]
+    ordinal = jnp.cumsum(my_remote.astype(jnp.int32)) - 1
+    compact_ids = jnp.arange(REM_DEV, dtype=jnp.int32)
+    compact_pick = my_remote[None, :] & (ordinal[None, :] == compact_ids[:, None])
+    compact_index = jnp.sum(jnp.where(compact_pick, flat_index[None, :], 0), axis=1)
+
+    split = FEATURE_SPLIT
+    if col_count % split or full_width % split:
+        split = 1
+    part = full_width // split
+    own_part = col_index % split
+    store_parts = group_store.reshape(slot_count, group_len, split, part)
+    my_store = lax.dynamic_index_in_dim(store_parts, own_part, 2, keepdims=False)
+    payload = my_store[send_slot]
     received = lax.all_to_all(
         jnp.where(send_live[:, :, None, None], payload, jnp.zeros_like(payload)),
         "row",
@@ -88,8 +101,14 @@
         concat_axis=0,
         tiled=True,
     )
-    flat = received.reshape((row_count * capacity,) + group_store.shape[1:])
-    far = flat[jnp.where(my_remote, flat_index, 0)]
+    flat = received.reshape(row_count * capacity, group_len, part)
+    compact = flat[compact_index]
+    pieces = [compact] + [
+        lax.ppermute(compact, "col", [(c, c ^ m) for c in range(col_count)]) for m in range(1, split)
+    ]
+    stacked = jnp.stack(pieces)[jnp.arange(split, dtype=jnp.int32) ^ own_part]
+    far_all = stacked.transpose(1, 2, 0, 3).reshape(REM_DEV, group_len, full_width)
+    far = far_all[jnp.clip(ordinal, 0, REM_DEV - 1)]
     near = group_store[my_slot]
     return jnp.where(my_remote[:, None, None], far, near)
 
@@ -110,7 +129,9 @@
     query_count = req_here * sel_count
 
     query_rows, keyval_rows, out_cols = gather_weights(w_query, w_keyval, w_out, row_count)
-    groups = fetch_groups(group_store, group_src, row_count, row_index, req_here)
+    groups = fetch_groups(
+        group_store, group_src, row_count, row_index, col_count, col_index, req_here
+    )
 
     pos_global = positions.astype(jnp.float32)
     pos_local = jnp.tile(pos_global[:group_len], (group_count, 1))

time: 367 us -> 306 us (0.83)
  the two profiles are of different devices: /device:TPU:1 before, /device:TPU:9 now
where the time goes in v2:
time: 306 us; the launch traced here: 305 us
  waiting for transfers between devices  111 us (36%)
  starting transfers between devices  80.3 us (26%)
  local copies, waits for them, and re-layouts  67.9 us (22%)
  other arithmetic  36.7 us (12%)
  matrix products  7.89 us (3%)
    ppermute x7, waiting for transfers between devices, row_gather(): lax.ppermute(stage, 'row', [(z * run + a, (z + s) % runs * run + a) for z...  50.4 us
    ppermute x3, waiting for transfers between devices, fetch_groups(): lax.ppermute(compact, 'col', [(c, c ^ m) for c in range(col_count)])  36.6 us
    ppermute x7, starting transfers between devices, row_gather(): lax.ppermute(stage, 'row', [(z * run + a, (z + s) % runs * run + a) for z...  23.3 us
    all_to_all x1, waiting for transfers between devices, per_device(): lax.all_to_all(projected, 'col', 0, 0, tiled=True)  22.9 us
    all_to_all x1, starting transfers between devices, per_device(): lax.all_to_all(projected, 'col', 0, 0, tiled=True)  18.4 us
    convert_element_type x2, other arithmetic, per_device(): normed = layer_norm(shifted, ln_gain).astype(jnp.bfloat16)  12.5 us
    all_to_all x1, starting transfers between devices, fetch_groups(): lax.all_to_all(jnp.where(send_live[:, :, None, None], payload, jnp.zeros_...  12.3 us
    ppermute x3, starting transfers between devices, row_gather(): lax.ppermute(block, 'row', [(z * run + a, z * run + (a + s) % run) for z...  10.4 us
  transfers between devices with their start and end apart: 17, of which 7 were waited for; matrix products, arithmetic and copies ran while one was open for 12% of the time, Pallas kernels for 0%

profile of v2, /device:TPU:9, one launch (start us, length us, event | category | flops | bytes accessed | tf_op | source)
XLA Modules:
  0.0 305.1 jit_solution(1280500477314877207)
XLA Ops:
  5.4 4.4 %collective-permute-start.4 = (bf16[20000]{0:T(1024)(128)(2,1)S(1)}, bf16[20000]{0:T(1024)(128)(2,1)S(1)}, u32[]{:S(2)}, u32[]{:S(2)}) collective-permute-start(bf16[20000]{0:T(1024)(128)(2,1)S(1)} %concatenate.7), channel_id=1, source_target_pairs={{0,32},{16,48},{32,0},{48,16},{64,96},{80,112},{96,64},{112,80},{1... | collective-permute-start | bytes 120008 | tf_op jit(solution)/shard_map/ppermute | solution.py:24
  9.8 4.1 %collective-permute-start.3 = (bf16[20000]{0:T(1024)(128)(2,1)S(1)}, bf16[20000]{0:T(1024)(128)(2,1)S(1)}, u32[]{:S(2)}, u32[]{:S(2)}) collective-permute-start(bf16[20000]{0:T(1024)(128)(2,1)S(1)} %concatenate.7), channel_id=1, source_target_pairs={{0,16},{16,32},{32,48},{48,0},{64,80},{80,96},{96,112},{112,64},{1... | collective-permute-start | bytes 120008 | tf_op jit(solution)/shard_map/ppermute | solution.py:24
  15.6 6.5 %reshape.491 = bf16[16,32,4,400]{3,2,1,0:T(4,128)(2,1)S(1)} reshape(bf16[16,32,1600]{2,1,0:T(8,128)(2,1)} %param.9) | data formatting | bytes 3276800 | tf_op jit(solution)/shard_map/reshape | solution.py:94
  25.7 12.3 %all-to-all-start = ((bf16[32,2,32,400]{3,2,1,0:T(8,128)(2,1)}), bf16[32,2,32,400]{3,2,1,0:T(8,128)(2,1)}, u32[]{:S(2)}, u32[]{:S(2)}) async-start(bf16[32,2,32,400]{3,2,1,0:T(8,128)(2,1)} %broadcast_select_fusion), calls=%async_computation | async-start | bytes 4194304 | tf_op jit(solution)/shard_map/all_to_all | solution.py:97
  51.7 4.4 %collective-permute-start.11 = (bf16[4,20000]{1,0:T(4,128)(2,1)S(1)}, bf16[4,20000]{1,0:T(4,128)(2,1)S(1)}, u32[]{:S(2)}, u32[]{:S(2)}) collective-permute-start(bf16[4,20000]{1,0:T(4,128)(2,1)S(1)} %get-tuple-element.30), channel_id=1, source_target_pairs={{0,384},{16,400},{32,416},{48,432},{64,448},{80,464},{96,480},{112... | collective-permute-start | bytes 480008 | tf_op jit(solution)/shard_map/ppermute | solution.py:29
  56.1 6.0 %collective-permute-start.10 = (bf16[4,20000]{1,0:T(4,128)(2,1)S(1)}, bf16[4,20000]{1,0:T(4,128)(2,1)S(1)}, u32[]{:S(2)}, u32[]{:S(2)}) collective-permute-start(bf16[4,20000]{1,0:T(4,128)(2,1)S(1)} %get-tuple-element.30), channel_id=1, source_target_pairs={{0,320},{16,336},{32,352},{48,368},{64,384},{80,400},{96,416},{112... | collective-permute-start | bytes 480008 | tf_op jit(solution)/shard_map/ppermute | solution.py:29
  64.3 3.7 %collective-permute-start.8 = (bf16[4,20000]{1,0:T(4,128)(2,1)S(1)}, bf16[4,20000]{1,0:T(4,128)(2,1)S(1)}, u32[]{:S(2)}, u32[]{:S(2)}) collective-permute-start(bf16[4,20000]{1,0:T(4,128)(2,1)S(1)} %get-tuple-element.30), channel_id=1, source_target_pairs={{0,192},{16,208},{32,224},{48,240},{64,256},{80,272},{96,288},{112... | collective-permute-start | bytes 480008 | tf_op jit(solution)/shard_map/ppermute | solution.py:29
  68.0 23.9 %collective-permute-done.6 = bf16[4,20000]{1,0:T(4,128)(2,1)S(1)} collective-permute-done((bf16[4,20000]{1,0:T(4,128)(2,1)S(1)}, bf16[4,20000]{1,0:T(4,128)(2,1)S(1)}, u32[]{:S(2)}, u32[]{:S(2)}) %collective-permute-start.6) | collective-permute-done | bytes 160032 | tf_op jit(solution)/shard_map/ppermute | solution.py:29
  93.9 23.0 %collective-permute-done.7 = bf16[4,20000]{1,0:T(4,128)(2,1)S(1)} collective-permute-done((bf16[4,20000]{1,0:T(4,128)(2,1)S(1)}, bf16[4,20000]{1,0:T(4,128)(2,1)S(1)}, u32[]{:S(2)}, u32[]{:S(2)}) %collective-permute-start.7) | collective-permute-done | bytes 160032 | tf_op jit(solution)/shard_map/ppermute | solution.py:29
  135.0 5.1 %collective-permute-start = (bf16[32,32,400]{2,1,0:T(8,128)(2,1)S(1)}, bf16[32,32,400]{2,1,0:T(8,128)(2,1)}, u32[]{:S(2)}, u32[]{:S(2)}) collective-permute-start(bf16[32,32,400]{2,1,0:T(8,128)(2,1)S(1)} %gather_fusion.1), channel_id=1, source_target_pairs={{0,1},{1,0},{2,3},{3,2},{4,5},{5,4},{6,7},{7,6},{8,9},{9,8},{10,11... | collective-permute-start | bytes 2457608 | tf_op jit(solution)/shard_map/ppermute | solution.py:107
  144.6 10.9 %collective-permute-done.1 = bf16[32,32,400]{2,1,0:T(8,128)(2,1)} collective-permute-done((bf16[32,32,400]{2,1,0:T(8,128)(2,1)S(1)}, bf16[32,32,400]{2,1,0:T(8,128)(2,1)}, u32[]{:S(2)}, u32[]{:S(2)}) %collective-permute-start.1) | collective-permute-done | bytes 819232 | tf_op jit(solution)/shard_map/ppermute | solution.py:107
  155.6 25.7 %collective-permute-done.2 = bf16[32,32,400]{2,1,0:T(8,128)(2,1)} collective-permute-done((bf16[32,32,400]{2,1,0:T(8,128)(2,1)S(1)}, bf16[32,32,400]{2,1,0:T(8,128)(2,1)}, u32[]{:S(2)}, u32[]{:S(2)}) %collective-permute-start.2) | collective-permute-done | bytes 819232 | tf_op jit(solution)/shard_map/ppermute | solution.py:107
  181.2 3.7 %pad_maximum_fusion = bf16[4,32,32,400]{3,2,1,0:T(8,128)(2,1)} fusion(bf16[1,32,32,400]{3,2,1,0:T(8,128)(2,1)} %bitcast.13, bf16[1,32,32,400]{3,2,1,0:T(8,128)(2,1)} %bitcast.12, bf16[1,32,32,400]{3,2,1,0:T(8,128)(2,1)} %bitcast.11, bf16[1,32,32,400]{3,2,1,0:T(8,128)(2,1)S(1)} %bitcast.119), kind=kLoop, calls=%fused_computation.14 | loop fusion | flops 4915200 | bytes 6553600 | tf_op jit(solution)/shard_map/stack | solution.py:109
  184.9 5.0 %gather_fusion.2 = bf16[4,32,32,400]{3,2,1,0:T(8,128)(2,1)} fusion(bf16[4,32,32,400]{3,2,1,0:T(8,128)(2,1)} %pad_maximum_fusion, s32[1024]{0:T(1024)S(1)} %get-tuple-element.51), kind=kCustom, calls=%fused_computation.2 | custom fusion | bytes 6553616 | tf_op jit(solution)/shard_map/gather | solution.py:109
  189.9 8.1 %copy.80 = bf16[32,32,4,400]{3,2,1,0:T(4,128)(2,1)} copy(bf16[32,32,4,400]{3,1,0,2:T(8,128)(2,1)} %bitcast.114) | data formatting | bytes 6553600 | tf_op jit(solution)/shard_map/transpose | solution.py:110
  197.9 7.4 %reshape.493 = bf16[32,32,1600]{2,1,0:T(8,128)(2,1)S(1)} reshape(bf16[32,32,4,400]{3,2,1,0:T(4,128)(2,1)} %copy.80) | data formatting | bytes 6553600 | tf_op jit(solution)/shard_map/reshape | solution.py:110
  209.9 7.3 %fusion.62 = (f32[4,320]{1,0:T(4,128)S(1)}, f32[4,320,1600]{2,1,0:T(8,128)}) fusion(f32[320,1600]{1,0:T(8,128)S(1)} %bitcast.112, f32[320,1600]{1,0:T(8,128)} %convert_element_type.85, pred[4,320]{1,0:T(4,128)(4,1)S(1)} %broadcast_in_dim.188, bf16[4,320,1600]{2,1,0:T(8,128)(2,1)} %bitcast.104, bf16[4,320,1600]{2,1,0:T(8,128)(2,1)} %bitcast.107), kind=kLoop, calls=%fused_computation.161 | loop fusion | flops 10238720 | bytes 20486400 | tf_op jit(solution)/shard_map/reduce_sum | solution.py:15
  217.3 4.4 %multiply_reduce_fusion = f32[4,320]{1,0:T(4,128)S(1)} fusion(f32[4,320,1600]{2,1,0:T(8,128)} %get-tuple-element.32, f32[4,320]{1,0:T(4,128)S(1)} %broadcast_multiply_fusion), kind=kLoop, calls=%fused_computation.11 | loop fusion | flops 6142720 | bytes 8202240 | tf_op jit(solution)/shard_map/reduce_sum | solution.py:16
  221.8 5.5 %multiply_convert_fusion = bf16[4,320,1600]{2,1,0:T(8,128)(2,1)} fusion(f32[4,320,1600]{2,1,0:T(8,128)} %get-tuple-element.32, f32[1600]{0:T(1024)S(1)} %convert_element_type.87, f32[4,320]{1,0:T(4,128)S(1)} %add_rsqrt_fusion, f32[4,320]{1,0:T(4,128)S(1)} %broadcast_multiply_fusion), kind=kLoop, calls=%fused_computation.9 | loop fusion | flops 8192000 | bytes 12304640 | tf_op jit(solution)/shard_map/convert_element_type | solution.py:140
  231.6 4.1 %add.263 = f32[4,320,1600]{2,1,0:T(8,128)} broadcast(bf16[320,1600]{1,0:T(8,128)(2,1)S(1)} %copy-done.2), dimensions={1,2} | broadcast | bytes 9216000 | tf_op jit(solution)/shard_map/add | solution.py:139
  235.7 7.0 %multiply_convert_fusion.1 = bf16[40,32,1600]{2,1,0:T(8,128)(2,1)} fusion(f32[40,32,1600]{2,1,0:T(8,128)S(1)} %bitcast.110, f32[40,32,1600]{2,1,0:T(8,128)} %bitcast.111, f32[1600]{0:T(1024)S(1)} %convert_element_type.87, f32[40,32]{1,0:T(8,128)S(1)} %rsqrt.13, f32[40,32]{1,0:T(8,128)S(1)} %div.83, bf16[40,32,1600]{2,1,0:T(8,128)(2,1)S(1)} %bitcast.109, ...), kind=kLoop, calls=%fused_computation.10 | loop fusion | flops 16384000 | bytes 28689920 | tf_op jit(solution)/shard_map/convert_element_type | solution.py:140
  242.7 3.9 %fusion = bf16[4,320,2,100]{1,3,2,0:T(8,128)(2,1)S(1)} fusion(bf16[4,320,1600,1]{2,1,3,0:T(8,128)(2,1)} %bitcast.118, bf16[1600,2,100]{0,2,1:T(8,128)(2,1)S(1)} %copy-done.6, pred[4,320]{1,0:T(4,128)(4,1)S(1)} %iota_compare_fusion.5), kind=kOutput, calls=%fused_computation.18 | convolution fusion | flops 819712000 | bytes 5249280 | tf_op jit(solution)/shard_map/btd,dsc->btsc/dot_general | solution.py:146
  259.1 18.4 %all-to-all-start.1 = ((f32[16,128,100]{1,2,0:T(8,128)}), f32[16,128,100]{1,2,0:T(8,128)S(1)}, u32[]{:S(2)}, u32[]{:S(2)}) async-start(f32[16,128,100]{1,2,0:T(8,128)} %convolution_bitcast_fusion), calls=%async_computation.1 | async-start | bytes 1703936 | tf_op jit(solution)/shard_map/all_to_all | solution.py:195
  281.3 22.9 %all-to-all-done.1 = f32[16,128,100]{1,2,0:T(8,128)S(1)} async-done(((f32[16,128,100]{1,2,0:T(8,128)}), f32[16,128,100]{1,2,0:T(8,128)S(1)}, u32[]{:S(2)}, u32[]{:S(2)}) %all-to-all-start.1) | async-done | bytes 819232 | tf_op jit(solution)/shard_map/all_to_all | solution.py:195
  (168 shorter events, 76.1 us)
Async XLA Ops:
  3.5 37.9 %collective-permute-start.5 = (bf16[20000]{0:T(1024)(128)(2,1)S(1)}, bf16[20000]{0:T(1024)(128)(2,1)S(1)}, u32[]{:S(2)}, u32[]{:S(2)}) collective-permute-start(bf16[20000]{0:T(1024)(128)(2,1)S(1)} %concatenate.7), channel_id=1, source_target_pairs={{0,48},{16,0},{32,16},{48,32},{64,112},{80,64},{96,80},{112,96},{1... | collective-permute-start | bytes 120008 | tf_op jit(solution)/shard_map/ppermute | solution.py:24
  5.4 36.1 %collective-permute-start.4 = (bf16[20000]{0:T(1024)(128)(2,1)S(1)}, bf16[20000]{0:T(1024)(128)(2,1)S(1)}, u32[]{:S(2)}, u32[]{:S(2)}) collective-permute-start(bf16[20000]{0:T(1024)(128)(2,1)S(1)} %concatenate.7), channel_id=1, source_target_pairs={{0,32},{16,48},{32,0},{48,16},{64,96},{80,112},{96,64},{112,80},{1... | collective-permute-start | bytes 120008 | tf_op jit(solution)/shard_map/ppermute | solution.py:24
  9.8 31.8 %collective-permute-start.3 = (bf16[20000]{0:T(1024)(128)(2,1)S(1)}, bf16[20000]{0:T(1024)(128)(2,1)S(1)}, u32[]{:S(2)}, u32[]{:S(2)}) collective-permute-start(bf16[20000]{0:T(1024)(128)(2,1)S(1)} %concatenate.7), channel_id=1, source_target_pairs={{0,16},{16,32},{32,48},{48,0},{64,80},{80,96},{96,112},{112,64},{1... | collective-permute-start | bytes 120008 | tf_op jit(solution)/shard_map/ppermute | solution.py:24
  24.2 14.0 %copy-start.9 = (s32[32,4]{0,1:T(4,128)S(1)}, s32[32,4]{0,1:T(4,128)}, u32[]{:S(2)}) copy-start(s32[32,4]{0,1:T(4,128)} %param.16) | copy-start | bytes 1540
  24.2 16.0 %copy-start.7 = (s32[128,32]{0,1:T(8,128)S(1)}, s32[128,32]{0,1:T(8,128)}, u32[]{:S(2)}) copy-start(s32[128,32]{0,1:T(8,128)} %param.17) | copy-start | bytes 49156
  25.7 20.3 %copy-start.1 = (bf16[320,1600]{1,0:T(8,128)(2,1)S(1)}, bf16[320,1600]{1,0:T(8,128)(2,1)}, u32[]{:S(2)}) copy-start(bf16[320,1600]{1,0:T(8,128)(2,1)} %param.10) | copy-start | bytes 3072004
  25.7 22.5 %copy-start.8 = (bf16[1600]{0:T(1024)(128)(2,1)S(1)}, bf16[1600]{0:T(1024)(128)(2,1)}, u32[]{:S(2)}) copy-start(bf16[1600]{0:T(1024)(128)(2,1)} %param.11) | copy-start | bytes 9604
  25.7 22.6 %copy-start = (bf16[16,32,1600]{2,1,0:T(8,128)(2,1)S(1)}, bf16[16,32,1600]{2,1,0:T(8,128)(2,1)}, u32[]{:S(2)}) copy-start(bf16[16,32,1600]{2,1,0:T(8,128)(2,1)} %param.9) | copy-start | bytes 4915204
  25.7 103.9 %all-to-all-start = ((bf16[32,2,32,400]{3,2,1,0:T(8,128)(2,1)}), bf16[32,2,32,400]{3,2,1,0:T(8,128)(2,1)}, u32[]{:S(2)}, u32[]{:S(2)}) async-start(bf16[32,2,32,400]{3,2,1,0:T(8,128)(2,1)} %broadcast_select_fusion), calls=%async_computation | async-start | bytes 4194304 | tf_op jit(solution)/shard_map/all_to_all | solution.py:97
  42.6 49.2 %collective-permute-start.6 = (bf16[4,20000]{1,0:T(4,128)(2,1)S(1)}, bf16[4,20000]{1,0:T(4,128)(2,1)S(1)}, u32[]{:S(2)}, u32[]{:S(2)}) collective-permute-start(bf16[4,20000]{1,0:T(4,128)(2,1)S(1)} %get-tuple-element.30), channel_id=1, source_target_pairs={{0,64},{16,80},{32,96},{48,112},{64,128},{80,144},{96,160},{112,17... | collective-permute-start | bytes 480008 | tf_op jit(solution)/shard_map/ppermute | solution.py:29
  48.3 45.5 %copy-start.4 = (bf16[8,4,20000]{2,1,0:T(4,128)(2,1)S(1)}, bf16[8,4,20000]{2,1,0:T(4,128)(2,1)}, u32[]{:S(2)}) copy-start(bf16[8,4,20000]{2,1,0:T(4,128)(2,1)} %get-tuple-element.29) | copy-start | bytes 3840004
  51.7 67.6 %collective-permute-start.11 = (bf16[4,20000]{1,0:T(4,128)(2,1)S(1)}, bf16[4,20000]{1,0:T(4,128)(2,1)S(1)}, u32[]{:S(2)}, u32[]{:S(2)}) collective-permute-start(bf16[4,20000]{1,0:T(4,128)(2,1)S(1)} %get-tuple-element.30), channel_id=1, source_target_pairs={{0,384},{16,400},{32,416},{48,432},{64,448},{80,464},{96,480},{112... | collective-permute-start | bytes 480008 | tf_op jit(solution)/shard_map/ppermute | solution.py:29
  56.1 63.2 %collective-permute-start.10 = (bf16[4,20000]{1,0:T(4,128)(2,1)S(1)}, bf16[4,20000]{1,0:T(4,128)(2,1)S(1)}, u32[]{:S(2)}, u32[]{:S(2)}) collective-permute-start(bf16[4,20000]{1,0:T(4,128)(2,1)S(1)} %get-tuple-element.30), channel_id=1, source_target_pairs={{0,320},{16,336},{32,352},{48,368},{64,384},{80,400},{96,416},{112... | collective-permute-start | bytes 480008 | tf_op jit(solution)/shard_map/ppermute | solution.py:29
  62.1 57.1 %collective-permute-start.9 = (bf16[4,20000]{1,0:T(4,128)(2,1)S(1)}, bf16[4,20000]{1,0:T(4,128)(2,1)S(1)}, u32[]{:S(2)}, u32[]{:S(2)}) collective-permute-start(bf16[4,20000]{1,0:T(4,128)(2,1)S(1)} %get-tuple-element.30), channel_id=1, source_target_pairs={{0,256},{16,272},{32,288},{48,304},{64,320},{80,336},{96,352},{112... | collective-permute-start | bytes 480008 | tf_op jit(solution)/shard_map/ppermute | solution.py:29
  64.3 54.8 %collective-permute-start.8 = (bf16[4,20000]{1,0:T(4,128)(2,1)S(1)}, bf16[4,20000]{1,0:T(4,128)(2,1)S(1)}, u32[]{:S(2)}, u32[]{:S(2)}) collective-permute-start(bf16[4,20000]{1,0:T(4,128)(2,1)S(1)} %get-tuple-element.30), channel_id=1, source_target_pairs={{0,192},{16,208},{32,224},{48,240},{64,256},{80,272},{96,288},{112... | collective-permute-start | bytes 480008 | tf_op jit(solution)/shard_map/ppermute | solution.py:29
  91.9 25.0 %collective-permute-start.7 = (bf16[4,20000]{1,0:T(4,128)(2,1)S(1)}, bf16[4,20000]{1,0:T(4,128)(2,1)S(1)}, u32[]{:S(2)}, u32[]{:S(2)}) collective-permute-start(bf16[4,20000]{1,0:T(4,128)(2,1)S(1)} %get-tuple-element.30), channel_id=1, source_target_pairs={{0,128},{16,144},{32,160},{48,176},{64,192},{80,208},{96,224},{112... | collective-permute-start | bytes 480008 | tf_op jit(solution)/shard_map/ppermute | solution.py:29
  116.9 6.0 %collective-permute-start.12 = (bf16[4,20000]{1,0:T(4,128)(2,1)S(1)}, bf16[4,20000]{1,0:T(4,128)(2,1)S(1)}, u32[]{:S(2)}, u32[]{:S(2)}) collective-permute-start(bf16[4,20000]{1,0:T(4,128)(2,1)S(1)} %get-tuple-element.30), channel_id=1, source_target_pairs={{0,448},{16,464},{32,480},{48,496},{64,0},{80,16},{96,32},{112,48}... | collective-permute-start | bytes 480008 | tf_op jit(solution)/shard_map/ppermute | solution.py:29
  131.9 23.7 %collective-permute-start.1 = (bf16[32,32,400]{2,1,0:T(8,128)(2,1)S(1)}, bf16[32,32,400]{2,1,0:T(8,128)(2,1)}, u32[]{:S(2)}, u32[]{:S(2)}) collective-permute-start(bf16[32,32,400]{2,1,0:T(8,128)(2,1)S(1)} %gather_fusion.1), channel_id=1, source_target_pairs={{0,2},{1,3},{2,0},{3,1},{4,6},{5,7},{6,4},{7,5},{8,10},{9,11},{10,... | collective-permute-start | bytes 2457608 | tf_op jit(solution)/shard_map/ppermute | solution.py:107
  135.0 20.6 %collective-permute-start = (bf16[32,32,400]{2,1,0:T(8,128)(2,1)S(1)}, bf16[32,32,400]{2,1,0:T(8,128)(2,1)}, u32[]{:S(2)}, u32[]{:S(2)}) collective-permute-start(bf16[32,32,400]{2,1,0:T(8,128)(2,1)S(1)} %gather_fusion.1), channel_id=1, source_target_pairs={{0,1},{1,0},{2,3},{3,2},{4,5},{5,4},{6,7},{7,6},{8,9},{9,8},{10,11... | collective-permute-start | bytes 2457608 | tf_op jit(solution)/shard_map/ppermute | solution.py:107
  140.1 41.1 %collective-permute-start.2 = (bf16[32,32,400]{2,1,0:T(8,128)(2,1)S(1)}, bf16[32,32,400]{2,1,0:T(8,128)(2,1)}, u32[]{:S(2)}, u32[]{:S(2)}) collective-permute-start(bf16[32,32,400]{2,1,0:T(8,128)(2,1)S(1)} %gather_fusion.1), channel_id=1, source_target_pairs={{0,3},{1,2},{2,1},{3,0},{4,7},{5,6},{6,5},{7,4},{8,11},{9,10},{10,... | collective-permute-start | bytes 2457608 | tf_op jit(solution)/shard_map/ppermute | solution.py:107
  242.7 10.4 %copy-start.5 = (bf16[32,5000]{1,0:T(8,128)(2,1)S(1)}, bf16[32,5000]{1,0:T(8,128)(2,1)}, u32[]{:S(2)}) copy-start(bf16[32,5000]{1,0:T(8,128)(2,1)} %get-tuple-element.37) | copy-start | bytes 960004
  247.2 7.5 %collective-permute-start.13 = (f32[4,32,320]{2,1,0:T(8,128)S(1)}, f32[4,32,320]{2,1,0:T(8,128)S(1)}, u32[]{:S(2)}, u32[]{:S(2)}) collective-permute-start(f32[4,32,320]{2,1,0:T(8,128)S(1)} %fusion.9), channel_id=1, source_target_pairs={{1,0},{2,1},{3,2},{4,3},{5,4},{6,5},{7,6},{8,7},{9,8},{10,9},{11,1... | collective-permute-start | bytes 491528 | tf_op jit(solution)/shard_map/ppermute | solution.py:177
  249.4 6.2 %collective-permute-start.14 = (f32[4,32,320]{2,1,0:T(8,128)S(1)}, f32[4,32,320]{2,1,0:T(8,128)S(1)}, u32[]{:S(2)}, u32[]{:S(2)}) collective-permute-start(f32[4,32,320]{2,1,0:T(8,128)S(1)} %get-tuple-element.46), channel_id=1, source_target_pairs={{0,1},{1,2},{2,3},{3,4},{4,5},{5,6},{6,7},{7,8},{8,9},{9,10},{10,1... | collective-permute-start | bytes 491528 | tf_op jit(solution)/shard_map/ppermute | solution.py:176
  259.1 45.2 %all-to-all-start.1 = ((f32[16,128,100]{1,2,0:T(8,128)}), f32[16,128,100]{1,2,0:T(8,128)S(1)}, u32[]{:S(2)}, u32[]{:S(2)}) async-start(f32[16,128,100]{1,2,0:T(8,128)} %convolution_bitcast_fusion), calls=%async_computation.1 | async-start | bytes 1703936 | tf_op jit(solution)/shard_map/all_to_all | solution.py:195
  (7 other events, 41.5 us)
